TPU v7x, 32 devices: a whole 2x2x4 slice. The times are simulated.
32 devices in a mesh: fsdp: 8 (over y, x, core), dp: 4 (over z).
Axes of the slice: x: 2, y: 2, z: 4, core: 2. Of those that a mesh axis runs over, the one named last changes fastest.
Arguments:
- tokens: bfloat16 [131072, 1024], P(('fsdp', 'dp')), may hold values from -6 to 6
- cotangent: bfloat16 [131072, 1024], P(('fsdp', 'dp')), may hold values from -6 to 6
- lengths: int32 [256], P(('fsdp', 'dp')), may hold values from 8 to 2048, as said below
- selected: int32 [16384], P(('fsdp', 'dp')), may hold values from 0 to 4095, as said below
- attn_in: bfloat16 [1024, 3072], P('fsdp'), may hold values from -0.1875 to 0.1875
- attn_out: bfloat16 [1024, 1024], P('fsdp'), may hold values from -0.75 to 0.75
- mlp_in: bfloat16 [1024, 4096], P('fsdp'), may hold values from -0.1875 to 0.1875
- mlp_out: bfloat16 [4096, 1024], P('fsdp'), may hold values from -0.09375 to 0.09375
- norm_attn: bfloat16 [1024], P('fsdp'), may hold values from 0.5 to 1.5
- norm_mlp: bfloat16 [1024], P('fsdp'), may hold values from 0.5 to 1.5
- router: bfloat16 [1024], replicated, may hold values from -0.1875 to 0.1875
Outputs:
- output: bfloat16 [131072, 1024], P(('fsdp', 'dp'))
- grad_tokens: bfloat16 [131072, 1024], P(('fsdp', 'dp'))
- grad_attn_in: float32 [1024, 3072], P('fsdp')
- grad_attn_out: float32 [1024, 1024], P('fsdp')
- grad_mlp_in: float32 [1024, 4096], P('fsdp')
- grad_mlp_out: float32 [4096, 1024], P('fsdp')
- grad_norm_attn: float32 [1024], P('fsdp')
- grad_norm_mlp: float32 [1024], P('fsdp')
- grad_router: float32 [1024], replicated
Inputs may be any that keep to these rules, and one draw needn't show every extreme that they name: `lengths`: each aligned block of 8 entries (one device's sequences, in order) holds multiples of 8 that sum to 4096; exactly one of them equals 2048. `selected`: each aligned block of 512 entries lists distinct positions within its device's 4096 tokens in ascending order; a sequence of length L has exactly L / 8 of its positions listed.
All inputs are finite; a program needn't handle non-finite values.
Results may differ from a plain program's by a relative error of at most 0.014.
Values may be sent and summed in bfloat16 or wider, within the bound.
No kernel may reach another device: no remote copies, remote signals or barrier semaphores. Data moves between devices by JAX's collectives and lax.ppermute only.
A program may use at most 192 MiB of HBM per device.

v0:
```python
import jax
import jax.numpy as jnp
from jax import lax
from jax.sharding import PartitionSpec as P

HEADS = 16
HEAD = 64


EPS = 1e-06
MASKED = -1e30


def rms_scale(values, gain_vec):
    return values * lax.rsqrt(jnp.mean(values * values, axis=-1, keepdims=True) + EPS) * gain_vec


def seq_mask(lengths, selected):
    seq_ends = jnp.cumsum(lengths)
    owner_seq = jnp.sum((selected[:, None] >= seq_ends[None, :]).astype(jnp.int32), axis=1)
    return (owner_seq[:, None] == owner_seq[None, :]) & (selected[None, :] <= selected[:, None])


def split_heads(matrix):
    return matrix.reshape(matrix.shape[0], HEADS, HEAD)


def masked_scores(query_heads, key_heads, allowed, score_scale):
    scores = (
        jnp.einsum("qhd,khd->hqk", query_heads, key_heads, preferred_element_type=jnp.float32)
        * score_scale
    )
    return jnp.where(allowed[None], scores, MASKED)


def per_device(
    tokens,
    cotangent,
    lengths,
    selected,
    attn_in,
    attn_out,
    mlp_in,
    mlp_out,
    norm_attn,
    norm_mlp,
    router,
):
    model_width = tokens.shape[1]
    row_count = selected.shape[0]
    score_scale = HEAD ** (-0.5)
    w_qkv, w_out, gain_attn, gain_mlp = (
        lax.all_gather(attn_in, "fsdp", axis=0, tiled=True),
        lax.all_gather(attn_out, "fsdp", axis=0, tiled=True),
        lax.all_gather(norm_attn, "fsdp", axis=0, tiled=True),
        lax.all_gather(norm_mlp, "fsdp", axis=0, tiled=True),
    )
    w_in, w_down = (
        lax.all_gather(mlp_in, "fsdp", axis=0, tiled=True),
        lax.all_gather(mlp_out, "fsdp", axis=0, tiled=True),
    )
    gain_one = gain_attn.astype(jnp.float32)
    gain_two = gain_mlp.astype(jnp.float32)
    positions = lax.broadcasted_iota(jnp.int32, (row_count, tokens.shape[0]), 1)
    select = (selected[:, None] == positions).astype(jnp.bfloat16)
    routed = jnp.dot(select, tokens, preferred_element_type=jnp.float32)
    routed_low = routed.astype(jnp.bfloat16)
    router_rate = jnp.dot(routed_low, router, preferred_element_type=jnp.float32)
    allowed = seq_mask(lengths, selected)
    normed_float, norm_pull = jax.vjp(rms_scale, routed, gain_one)
    normed = normed_float.astype(jnp.bfloat16)
    qkv = jnp.dot(normed, w_qkv, preferred_element_type=jnp.float32).astype(jnp.bfloat16)
    query_heads = split_heads(qkv[:, :model_width])
    key_heads = split_heads(qkv[:, model_width : 2 * model_width])
    value_heads = split_heads(qkv[:, 2 * model_width :])
    scores = masked_scores(query_heads, key_heads, allowed, score_scale)
    highest = jnp.max(scores, axis=-1, keepdims=True)
    exponent = jnp.exp(scores - highest)
    row_total = jnp.sum(exponent, axis=-1, keepdims=True)
    probabilities = (exponent / row_total).astype(jnp.bfloat16)
    log_total = highest + jnp.log(row_total)
    attn_mix = jnp.einsum(
        "hqk,khd->qhd", probabilities, value_heads, preferred_element_type=jnp.float32
    )
    attn_mix = attn_mix.reshape(row_count, model_width).astype(jnp.bfloat16)
    attended = jnp.dot(attn_mix, w_out, preferred_element_type=jnp.float32)
    middle = routed + attended
    normed_two_float, middle_pull = jax.vjp(rms_scale, middle, gain_two)
    normed_two = normed_two_float.astype(jnp.bfloat16)
    pre_gelu = jnp.dot(normed_two, w_in, preferred_element_type=jnp.float32)
    active_float, gelu_pull = jax.vjp(jax.nn.gelu, pre_gelu)
    active = active_float.astype(jnp.bfloat16)
    expanded = jnp.dot(active, w_down, preferred_element_type=jnp.float32)
    update = attended + expanded
    branch = (router_rate[:, None] * update).astype(jnp.bfloat16)
    output = (
        tokens.astype(jnp.float32)
        + jnp.einsum("kt,kd->td", select, branch, preferred_element_type=jnp.float32)
    ).astype(jnp.bfloat16)
    w_qkv_back, w_out_back = (
        lax.all_gather(attn_in, "fsdp", axis=0, tiled=True),
        lax.all_gather(attn_out, "fsdp", axis=0, tiled=True),
    )
    w_in_back, w_down_back = (
        lax.all_gather(mlp_in, "fsdp", axis=0, tiled=True),
        lax.all_gather(mlp_out, "fsdp", axis=0, tiled=True),
    )
    cot_rows = jnp.dot(select, cotangent, preferred_element_type=jnp.float32)
    grad_rate = jnp.sum(cot_rows * update, axis=-1)
    grad_update = cot_rows * router_rate[:, None]
    grad_expanded = grad_update.astype(jnp.bfloat16)
    grad_down = jnp.einsum("kf,kd->fd", active, grad_expanded, preferred_element_type=jnp.float32)
    grad_active = jnp.einsum(
        "kd,fd->kf", grad_expanded, w_down_back, preferred_element_type=jnp.float32
    )
    (grad_inner_float,) = gelu_pull(grad_active)
    grad_inner = grad_inner_float.astype(jnp.bfloat16)
    grad_up = jnp.einsum("kd,kf->df", normed_two, grad_inner, preferred_element_type=jnp.float32)
    grad_normed_two = jnp.einsum(
        "kf,df->kd", grad_inner, w_in_back, preferred_element_type=jnp.float32
    )
    grad_middle, grad_gain_two = middle_pull(grad_normed_two)
    grad_attended = (grad_update + grad_middle).astype(jnp.bfloat16)
    grad_proj = jnp.einsum("ka,kd->ad", attn_mix, grad_attended, preferred_element_type=jnp.float32)
    grad_mix = jnp.einsum(
        "kd,ad->ka", grad_attended, w_out_back, preferred_element_type=jnp.float32
    ).astype(jnp.bfloat16)
    grad_mix_heads = split_heads(grad_mix)
    scores_again = masked_scores(query_heads, key_heads, allowed, score_scale)
    prob_float = jnp.where(allowed[None], jnp.exp(scores_again - log_total), 0.0)
    grad_probs = jnp.einsum(
        "qhd,khd->hqk", grad_mix_heads, value_heads, preferred_element_type=jnp.float32
    )
    row_delta = jnp.sum(prob_float * grad_probs, axis=-1, keepdims=True)
    grad_scores = (prob_float * (grad_probs - row_delta)).astype(jnp.bfloat16)
    prob_low = prob_float.astype(jnp.bfloat16)
    grad_query = (
        jnp.einsum("hqk,khd->qhd", grad_scores, key_heads, preferred_element_type=jnp.float32)
        * score_scale
    )
    grad_key = (
        jnp.einsum("hqk,qhd->khd", grad_scores, query_heads, preferred_element_type=jnp.float32)
        * score_scale
    )
    grad_value = jnp.einsum(
        "hqk,qhd->khd", prob_low, grad_mix_heads, preferred_element_type=jnp.float32
    )
    grad_qkv = jnp.concatenate(
        [
            grad_query.reshape(row_count, model_width),
            grad_key.reshape(row_count, model_width),
            grad_value.reshape(row_count, model_width),
        ],
        axis=1,
    ).astype(jnp.bfloat16)
    grad_proj_in = jnp.einsum("kd,ke->de", normed, grad_qkv, preferred_element_type=jnp.float32)
    grad_normed = jnp.einsum("ke,de->kd", grad_qkv, w_qkv_back, preferred_element_type=jnp.float32)
    grad_routed_norm, grad_gain_one = norm_pull(grad_normed)
    grad_routed = (
        grad_routed_norm + grad_middle + grad_rate[:, None] * router.astype(jnp.float32)
    ).astype(jnp.bfloat16)
    grad_tokens = (
        cotangent.astype(jnp.float32)
        + jnp.einsum("kt,kd->td", select, grad_routed, preferred_element_type=jnp.float32)
    ).astype(jnp.bfloat16)
    router_local = jnp.dot(grad_rate, routed, precision=lax.Precision.HIGHEST)
    shard_up, shard_down, shard_gain_two = (
        lax.psum_scatter(grad_up, "fsdp", scatter_dimension=0, tiled=True),
        lax.psum_scatter(grad_down, "fsdp", scatter_dimension=0, tiled=True),
        lax.psum_scatter(grad_gain_two, "fsdp", scatter_dimension=0, tiled=True),
    )
    shard_qkv, shard_proj, shard_gain_one = (
        lax.psum_scatter(grad_proj_in, "fsdp", scatter_dimension=0, tiled=True),
        lax.psum_scatter(grad_proj, "fsdp", scatter_dimension=0, tiled=True),
        lax.psum_scatter(grad_gain_one, "fsdp", scatter_dimension=0, tiled=True),
    )
    summed = (
        lax.psum(shard_qkv.astype(jnp.bfloat16), "dp").astype(jnp.float32),
        lax.psum(shard_proj.astype(jnp.bfloat16), "dp").astype(jnp.float32),
        lax.psum(shard_up.astype(jnp.bfloat16), "dp").astype(jnp.float32),
        lax.psum(shard_down.astype(jnp.bfloat16), "dp").astype(jnp.float32),
        lax.psum(shard_gain_one.astype(jnp.bfloat16), "dp").astype(jnp.float32),
        lax.psum(shard_gain_two.astype(jnp.bfloat16), "dp").astype(jnp.float32),
    )
    grad_router = lax.psum(router_local, ("fsdp", "dp"))
    return (
        output,
        grad_tokens,
        summed[0],
        summed[1],
        summed[2],
        summed[3],
        summed[4],
        summed[5],
        grad_router,
    )


def solution(mesh):
    placed = (
        P(("fsdp", "dp"), None),
        P(("fsdp", "dp"), None),
        P(("fsdp", "dp")),
        P(("fsdp", "dp")),
        P("fsdp", None),
        P("fsdp", None),
        P("fsdp", None),
        P("fsdp", None),
        P("fsdp"),
        P("fsdp"),
        P(),
    )
    return jax.shard_map(
        per_device,
        mesh=mesh,
        in_specs=placed,
        out_specs=(
            P(("fsdp", "dp"), None),
            P(("fsdp", "dp"), None),
            P("fsdp", None),
            P("fsdp", None),
            P("fsdp", None),
            P("fsdp", None),
            P("fsdp"),
            P("fsdp"),
            P(),
        ),
        check_vma=False,
    )
```

profile of v0, /device:TPU:0, one launch (start us, length us, event | category | flops | bytes accessed | tf_op | source)
XLA Modules:
  0.0 774.1 jit_solution(13917479941379814595)
XLA Ops:
  10.0 10.4 %all-gather = bf16[8,1,128]{2,1,0:T(2,128)(2,1)S(1)} all-gather(bf16[1,1,128]{2,1,0:T(2,128)(2,1)} %bitcast.84), channel_id=1, replica_groups=mesh['fsdp'=8,'dp'=4] {'fsdp'}, dimensions={0}, use_global_device_ids=true | all-gather | bytes 2304 | tf_op jit(solution)/shard_map/all_gather | solution.py:55
  20.4 8.9 %all-gather.1 = bf16[8,1,128]{2,1,0:T(2,128)(2,1)S(1)} all-gather(bf16[1,1,128]{2,1,0:T(2,128)(2,1)} %bitcast.85), channel_id=1, replica_groups=mesh['fsdp'=8,'dp'=4] {'fsdp'}, dimensions={0}, use_global_device_ids=true | all-gather | bytes 2304 | tf_op jit(solution)/shard_map/all_gather | solution.py:56
  40.1 9.3 %fusion.12 = f32[512,1024]{1,0:T(8,128)} fusion(bf16[4096,1024]{1,0:T(8,128)(2,1)} %param.12, s32[512]{0:T(512)S(1)} %copy-done.10), kind=kOutput, calls=%fused_computation.24 | convolution fusion | flops 4297064448 | bytes 10487808 | tf_op jit(solution)/shard_map/dot_general | solution.py:108
  81.2 9.3 %fusion = f32[16,512]{1,0:T(8,128)S(1)} fusion(f32[16,512,512]{1,2,0:T(8,128)} %get-tuple-element.31, f32[16,512]{1,0:T(8,128)S(1)} %get-tuple-element.30, pred[512,512]{0,1:T(8,128)(4,1)S(1)} %compare_and_fusion), kind=kLoop, calls=%fused_computation.8 | loop fusion | flops 16769024 | bytes 17104896 | tf_op jit(solution)/shard_map/reduce_sum | solution.py:79
  90.5 9.4 %fusion.23 = bf16[16,64,512]{2,1,0:T(8,128)(2,1)} fusion(bf16[512,16,64]{0,2,1:T(8,128)(2,1)} %bitcast.65, f32[16,512,512]{1,2,0:T(8,128)} %get-tuple-element.31, f32[16,512]{1,0:T(8,128)S(1)} %fusion, f32[16,512]{1,0:T(8,128)S(1)} %get-tuple-element.30, pred[512,512]{0,1:T(8,128)(4,1)S(1)} %compare_and_fusion), kind=kOutput, calls=%fused_computation.54 | convolution fusion | flops 558366720 | bytes 19202048 | tf_op jit(solution)/shard_map/hqk,khd->qhd/dot_general | solution.py:82
  105.2 38.7 %all-gather.11.cloned.1.call-done = bf16[1024,4096]{1,0:T(8,128)(2,1)} async-done(((bf16[128,4096]{1,0:T(8,128)(2,1)}), bf16[1024,4096]{1,0:T(8,128)(2,1)}) %all-gather.11.cloned.1.call-update) | async-done | bytes 8388624 | tf_op jit(solution)/shard_map/all_gather | solution.py:59
  143.9 12.1 %fusion.50 = f32[512,4096]{1,0:T(8,128)} fusion(bf16[1024,4096]{1,0:T(8,128)(2,1)} %all-gather.11.cloned.1.call-done, f32[512,1024]{1,0:T(8,128)} %get-tuple-element.22, f32[1024]{0:T(1024)S(1)} %bitcast.74, f32[512]{0:T(512)S(1)} %fusion.39), kind=kOutput, calls=%fused_computation.88 | convolution fusion | flops 4296540160 | bytes 18880512 | tf_op jit(solution)/shard_map/dot_general | solution.py:90
  156.0 44.0 %all-gather.13.cloned.1.call-done = bf16[4096,1024]{1,0:T(8,128)(2,1)} async-done(((bf16[512,1024]{1,0:T(8,128)(2,1)}), bf16[4096,1024]{1,0:T(8,128)(2,1)}) %all-gather.13.cloned.1.call-update) | async-done | bytes 8388624 | tf_op jit(solution)/shard_map/all_gather | solution.py:60
  200.0 14.6 %fusion.8 = bf16[512,4096]{1,0:T(8,128)(2,1)} fusion(f32[512,4096]{1,0:T(8,128)} %fusion.50, bf16[4096,1024]{1,0:T(8,128)(2,1)} %all-gather.13.cloned.1.call-done, f32[512,1024]{1,0:T(8,128)} %fusion.12, f32[512]{0:T(512)S(1)} %bitcast.79), kind=kOutput, calls=%fused_computation.18 | convolution fusion | flops 4337958912 | bytes 23070720 | tf_op jit(solution)/shard_map/kd,fd->kf/dot_general | solution.py:113
  214.6 10.9 %multiply_reduce_fusion.1 = (f32[1024]{0:T(1024)S(1)}, f32[512]{0:T(512)S(1)}, f32[512,1024]{1,0:T(8,128)}) fusion(f32[512,1024]{1,0:T(8,128)S(1)} %copy-done.1, f32[512]{0:T(512)S(1)} %fusion.39, f32[1024]{0:T(1024)S(1)} %bitcast.75, bf16[512,4096]{1,0:T(8,128)(2,1)} %fusion.8, bf16[1024,4096]{1,0:T(8,128)(2,1)} %all-gather.11.cloned.1.call-done), kind=kOutput, calls=%fused_computation.39 | convolution fusion | flops 4298111488 | bytes 16789504 | tf_op jit(solution)/shard_map/kf,df->kd/dot_general | solution.py:119
  225.5 10.3 %multiply_reduce_fusion.3 = (f32[512]{0:T(512)S(1)}, bf16[512,1024]{1,0:T(8,128)(2,1)S(1)}, f32[512,1024]{1,0:T(8,128)}) fusion(f32[512,1024]{1,0:T(8,128)S(1)} %copy-done.19, f32[512,1024]{1,0:T(8,128)S(1)} %copy-done.1, f32[512]{0:T(512)S(1)} %multiply_multiply_fusion.3, f32[512]{0:T(512)S(1)} %fusion.39, f32[512,1024]{1,0:T(8,128)} %get-tuple-element.33, ...), kind=kOutput, calls=%fused_computation.41 | convolution fusion | flops 4319608320 | bytes 28323840 | tf_op jit(solution)/shard_map/dot_general | solution.py:93
  246.6 13.6 %multiply_reduce_fusion = (f32[16,512]{1,0:T(8,128)S(1)}, f32[16,512,512]{1,2,0:T(8,128)}) fusion(f32[16,512]{1,0:T(8,128)S(1)} %log_add_fusion, f32[16,512,512]{1,2,0:T(8,128)} %get-tuple-element.31, pred[512,512]{0,1:T(8,128)(4,1)S(1)} %compare_and_fusion, bf16[512,16,64]{0,2,1:T(8,128)(2,1)} %bitcast.67, bf16[512,16,64]{0,2,1:T(8,128)(2,1)} %bitcast.66), kind=kOutput, calls=%fused_computation.2 | convolution fusion | flops 562028544 | bytes 35979264 | tf_op jit(solution)/shard_map/qhd,khd->hqk/dot_general | solution.py:131
  260.2 13.2 %multiply_convert_fusion = bf16[16,512,512]{1,2,0:T(8,128)(2,1)S(1)} fusion(f32[16,512,512]{1,2,0:T(8,128)} %get-tuple-element.36, f32[16,512]{1,0:T(8,128)S(1)} %get-tuple-element.35, f32[16,512]{1,0:T(8,128)S(1)} %log_add_fusion, f32[16,512,512]{1,2,0:T(8,128)} %get-tuple-element.31, pred[512,512]{0,1:T(8,128)(4,1)S(1)} %compare_and_fusion), kind=kLoop, calls=%fused_computation.1 | loop fusion | flops 29360128 | bytes 42270720 | tf_op jit(solution)/shard_map/convert_element_type | solution.py:135
  287.2 9.6 %fusion.27 = f32[1024,3072]{1,0:T(8,128)} fusion(bf16[512,1024]{0,1:T(8,128)(2,1)S(1)} %bitcast.88, bf16[512,1024]{0,1:T(8,128)(2,1)S(1)} %bitcast.63, bf16[512,1024]{0,1:T(8,128)(2,1)S(1)} %bitcast.59, f32[512,1024]{1,0:T(8,128)S(1)} %get-tuple-element.29, f32[1024]{0:T(1024)S(1)} %bitcast.71, f32[512]{0:T(512)S(1)} %fusion.38), kind=kOutput, calls=%fused_computation.57 | convolution fusion | flops 3232235520 | bytes 17831936 | tf_op jit(solution)/shard_map/kd,ke->de/dot_general | solution.py:156
  296.9 18.8 %fusion.47 = f32[4096,1024]{1,0:T(8,128)} fusion(f32[512,1024]{1,0:T(8,128)} %fusion.12, f32[512]{0:T(512)S(1)} %bitcast.81, f32[512,4096]{1,0:T(8,128)} %fusion.50), kind=kOutput, calls=%fused_computation.85 | convolution fusion | flops 4314890240 | bytes 27265024 | tf_op jit(solution)/shard_map/kf,kd->fd/dot_general | solution.py:112
  316.0 15.4 %fusion.49 = f32[1024,4096]{1,0:T(8,128)} fusion(bf16[512,4096]{1,0:T(8,128)(2,1)} %fusion.8, f32[512,1024]{1,0:T(8,128)} %get-tuple-element.22, f32[1024]{0:T(1024)S(1)} %bitcast.77, f32[512]{0:T(512)S(1)} %fusion.39), kind=kOutput, calls=%fused_computation.87 | convolution fusion | flops 4296540160 | bytes 23074816 | tf_op jit(solution)/shard_map/kd,kf->df/dot_general | solution.py:118
  341.8 15.9 %all-reduce.2 = (bf16[1024]{0:T(1024)(128)(2,1)S(1)}, bf16[1024]{0:T(1024)(128)(2,1)S(1)}) all-reduce(f32[1024]{0:T(1024)S(1)} %get-tuple-element.11, f32[1024]{0:T(1024)S(1)} %get-tuple-element.9), channel_id=6, replica_groups=mesh['fsdp'=8,'dp'=4] {'fsdp'}, use_global_device_ids=true, to_apply=%region_19.20.clone | all-reduce | flops 2048 | bytes 12288
  357.9 11.7 %all-reduce.3 = (bf16[128]{0:T(256)(128)(2,1)S(1)}, bf16[128]{0:T(256)(128)(2,1)S(1)}) all-reduce(bf16[128]{0:T(256)(128)(2,1)S(1)} %dynamic-slice.7, bf16[128]{0:T(256)(128)(2,1)S(1)} %dynamic-slice.6), channel_id=1, replica_groups=mesh['fsdp'=8,'dp'=4] {'dp'}, use_global_device_ids=true, to_apply=%region_20.21 | all-reduce | flops 256 | bytes 1024 | tf_op jit(solution)/shard_map/psum | solution.py:182
  371.7 37.7 %psum.55 = f32[1024]{0:T(1024)} all-reduce(f32[1024]{0:T(1024)S(1)} %bitcast.69), channel_id=1, replica_groups=mesh['fsdp'=8,'dp'=4] {'fsdp','dp'}, use_global_device_ids=true, to_apply=%region_24.25 | all-reduce | flops 1024 | bytes 8192 | tf_op jit(solution)/shard_map/psum | solution.py:185
  413.9 100.4 %reduce-scatter.11.cloned.1.call-done = f32[512,1024]{1,0:T(8,128)} async-done(((f32[4096,1024]{1,0:T(8,128)}), f32[512,1024]{1,0:T(8,128)}) %reduce-scatter.11.cloned.1.call-update) | async-done | bytes 2097168 | tf_op jit(solution)/shard_map/reduce_scatter | solution.py:169
  517.0 117.1 %reduce-scatter.9.cloned.1.call-done = f32[128,4096]{1,0:T(8,128)} async-done(((f32[1024,4096]{1,0:T(8,128)}), f32[128,4096]{1,0:T(8,128)}) %reduce-scatter.9.cloned.1.call-update) | async-done | bytes 2097168 | tf_op jit(solution)/shard_map/reduce_scatter | solution.py:168
  636.9 10.0 %add_convert_fusion.1 = bf16[4096,1024]{1,0:T(8,128)(2,1)} fusion(bf16[4096,1024]{1,0:T(8,128)(2,1)} %param.11, s32[512]{0:T(512)S(1)} %copy-done.11, f32[512,1024]{1,0:T(8,128)} %get-tuple-element.34, f32[512]{0:T(512)S(1)} %bitcast.82), kind=kOutput, calls=%fused_computation.4 | convolution fusion | flops 4310695936 | bytes 18878464 | tf_op jit(solution)/shard_map/kt,kd->td/dot_general | solution.py:98
  646.9 11.4 %add_convert_fusion = bf16[4096,1024]{1,0:T(8,128)(2,1)} fusion(bf16[4096,1024]{1,0:T(8,128)(2,1)} %param.12, s32[512]{0:T(512)S(1)} %copy-done.11, f32[512,1024]{1,0:T(8,128)S(1)} %get-tuple-element.29, f32[512,1024]{1,0:T(8,128)S(1)} %copy-done.20, f32[1024]{0:T(1024)S(1)} %convert_element_type.135, f32[512]{0:T(512)S(1)} %get-tuple-element.26, ...), kind=kOutput, calls=%fused_computation | convolution fusion | flops 4316987392 | bytes 25190400 | tf_op jit(solution)/shard_map/kt,kd->td/dot_general | solution.py:164
  658.3 100.1 %all-reduce.7.cloned.1.call-done = (bf16[128,3072]{1,0:T(8,128)(2,1)}, bf16[128,1024]{1,0:T(8,128)(2,1)}, bf16[128,4096]{1,0:T(8,128)(2,1)}, bf16[512,1024]{1,0:T(8,128)(2,1)}) async-done(((bf16[128,3072]{1,0:T(8,128)(2,1)}, bf16[128,1024]{1,0:T(8,128)(2,1)}, bf16[128,4096]{1,0:T(8,128)(2,1)}, bf16[512,1024]{1,0:T(8,128)(2,1)}), (bf16[128,3072]{1,0:T(8,128)(2,1)}, bf16[128,1024]{1,0:T(8,128)(2,1)}, ...) | async-done | bytes 3145744 | tf_op jit(solution)/shard_map/psum | solution.py:178
  (108 shorter events, 106.1 us)
Async XLA Ops:
  7.2 50.9 %all-gather.7.cloned.1.call-start = ((), (), s32[]{:S(2)}) async-start(), calls=%async_computation.4 | async-start | bytes 7077888 | tf_op jit(solution)/shard_map/all_gather | solution.py:53
  7.9 92.1 %all-gather.9.cloned.1.call-start = ((), (), s32[]{:S(2)}) async-start(), calls=%async_computation.5 | async-start | bytes 2359296 | tf_op jit(solution)/shard_map/all_gather | solution.py:54
  8.7 135.3 %all-gather.11.cloned.1.call-start = ((), (), s32[]{:S(2)}) async-start(), calls=%async_computation.6 | async-start | bytes 9437184 | tf_op jit(solution)/shard_map/all_gather | solution.py:59
  9.4 190.6 %all-gather.13.cloned.1.call-start = ((), (), s32[]{:S(2)}) async-start(), calls=%async_computation.7 | async-start | bytes 9437184 | tf_op jit(solution)/shard_map/all_gather | solution.py:60
  10.0 399.5 %reduce-scatter.7.cloned.1.call-start = ((), (), s32[]{:S(2)}) async-start(), calls=%async_computation.9 | async-start | bytes 4718592 | tf_op jit(solution)/shard_map/reduce_scatter | solution.py:174
  31.6 7.8 %copy-start.10 = (s32[512]{0:T(512)S(1)}, s32[512]{0:T(512)}, u32[]{:S(2)}) copy-start(s32[512]{0:T(512)} %param.14) | copy-start | bytes 6148
  200.0 14.7 %copy-start.1 = (f32[512,1024]{1,0:T(8,128)S(1)}, f32[512,1024]{1,0:T(8,128)}, u32[]{:S(2)}) copy-start(f32[512,1024]{1,0:T(8,128)} %get-tuple-element.22) | copy-start | bytes 6291460
  214.6 10.9 %copy-start.3 = (f32[512,1024]{1,0:T(8,128)S(1)}, f32[512,1024]{1,0:T(8,128)}, u32[]{:S(2)}) copy-start(f32[512,1024]{1,0:T(8,128)} %get-tuple-element.32) | copy-start | bytes 6291460
  214.6 10.9 %copy-start.15 = (bf16[4096,1024]{1,0:T(8,128)(2,1)S(1)}, bf16[4096,1024]{1,0:T(8,128)(2,1)}, u32[]{:S(2)}) copy-start(bf16[4096,1024]{1,0:T(8,128)(2,1)} %all-gather.13.cloned.1.call-done) | copy-start | bytes 25165828
  214.6 10.9 %copy-start.19 = (f32[512,1024]{1,0:T(8,128)S(1)}, f32[512,1024]{1,0:T(8,128)}, u32[]{:S(2)}) copy-start(f32[512,1024]{1,0:T(8,128)} %fusion.12) | copy-start | bytes 6291460
  225.5 11.3 %copy-start.6 = (bf16[16,64,512]{2,1,0:T(8,128)(2,1)S(1)}, bf16[16,64,512]{2,1,0:T(8,128)(2,1)}, u32[]{:S(2)}) copy-start(bf16[16,64,512]{2,1,0:T(8,128)(2,1)} %fusion.23) | copy-start | bytes 3145732
  246.5 164.8 %reduce-scatter.5.cloned.1.call-start = ((), (), s32[]{:S(2)}) async-start(), calls=%async_computation.8 | async-start | bytes 14155776 | tf_op jit(solution)/shard_map/reduce_scatter | solution.py:173
  260.2 13.2 %copy-start = (bf16[512,1024]{0,1:T(8,128)(2,1)S(1)}, bf16[512,1024]{0,1:T(8,128)(2,1)}, u32[]{:S(2)}) copy-start(bf16[512,1024]{0,1:T(8,128)(2,1)} %copy.49) | copy-start | bytes 3145732
  276.0 10.3 %copy-start.7 = (bf16[16,64,512]{2,1,0:T(8,128)(2,1)}, bf16[16,64,512]{2,1,0:T(8,128)(2,1)S(1)}, u32[]{:S(2)}) copy-start(bf16[16,64,512]{2,1,0:T(8,128)(2,1)S(1)} %multiply_convert_fusion.2) | copy-start | bytes 3145732
  277.6 8.7 %copy-start.4 = (bf16[16,64,512]{2,1,0:T(8,128)(2,1)}, bf16[16,64,512]{2,1,0:T(8,128)(2,1)S(1)}, u32[]{:S(2)}) copy-start(bf16[16,64,512]{2,1,0:T(8,128)(2,1)S(1)} %multiply_convert_fusion.3) | copy-start | bytes 3145732
  296.9 217.4 %reduce-scatter.11.cloned.1.call-start = ((), (), s32[]{:S(2)}) async-start(), calls=%async_computation.11 | async-start | bytes 18874368 | tf_op jit(solution)/shard_map/reduce_scatter | solution.py:169
  315.8 318.3 %reduce-scatter.9.cloned.1.call-start = ((), (), s32[]{:S(2)}) async-start(), calls=%async_computation.10 | async-start | bytes 18874368 | tf_op jit(solution)/shard_map/reduce_scatter | solution.py:168
  331.5 427.0 %all-reduce.7.cloned.1.call-start = ((), (), s32[]{:S(2)}) async-start(), calls=%async_computation.12 | async-start | bytes 6291456 | tf_op jit(solution)/shard_map/psum | solution.py:178
  333.4 76.0 %copy-start.14 = (f32[512]{0:T(512)S(1)}, f32[512]{0:T(512)}, u32[]{:S(2)}) copy-start(f32[512]{0:T(512)} %copy-done.13) | copy-start | bytes 6148
  409.4 227.4 %copy-start.11 = (s32[512]{0:T(512)S(1)}, s32[512]{0:T(512)}, u32[]{:S(2)}) copy-start(s32[512]{0:T(512)} %param.14) | copy-start | bytes 6148
  636.8 10.1 %copy-start.2 = (f32[512,1024]{1,0:T(8,128)S(1)}, f32[512,1024]{1,0:T(8,128)}, u32[]{:S(2)}) copy-start(f32[512,1024]{1,0:T(8,128)} %get-tuple-element.22) | copy-start | bytes 6291460
  636.8 10.1 %copy-start.20 = (f32[512,1024]{1,0:T(8,128)S(1)}, f32[512,1024]{1,0:T(8,128)}, u32[]{:S(2)}) copy-start(f32[512,1024]{1,0:T(8,128)} %get-tuple-element.37) | copy-start | bytes 6291460
  636.9 10.0 %copy-start.21 = (f32[512,1024]{1,0:T(8,128)S(1)}, f32[512,1024]{1,0:T(8,128)}, u32[]{:S(2)}) copy-start(f32[512,1024]{1,0:T(8,128)} %get-tuple-element.33) | copy-start | bytes 6291460
  758.4 7.1 copy-start.8
  (7 other events, 7.6 us)
Sparse Core Ops, SparseCore 0:
  9.9 48.1 all-gather.6
  59.9 27.7 all-gather.8
  89.6 54.2 all-gather.10
  145.7 54.2 all-gather.12
  246.7 51.1 reduce-scatter.6
  301.2 93.5 reduce-scatter.4
  398.4 115.8 reduce-scatter.10
  517.9 116.1 reduce-scatter.8
  637.3 121.0 all-reduce.6
where the time goes:
time: 783 us; the launch traced here: 774 us
  waiting for transfers between devices  412 us (53%)
  matrix products  204 us (26%)
  blocking collectives  84.6 us (11%)
  other arithmetic  44 us (6%)
  between operations  15.3 us (2%)
  local copies, waits for them, and re-layouts  14.3 us (2%)
    reduce_scatter x1, waiting for transfers between devices, per_device(): lax.psum_scatter(grad_up, 'fsdp', scatter_dimension=0, tiled=True)  117 us
    reduce_scatter x1, waiting for transfers between devices, per_device(): lax.psum_scatter(grad_down, 'fsdp', scatter_dimension=0, tiled=True)  100 us
    psum x1, waiting for transfers between devices, per_device(): lax.psum(shard_qkv.astype(jnp.bfloat16), 'dp').astype(jnp.float32)  100 us
    all_gather x1, waiting for transfers between devices, per_device(): lax.all_gather(mlp_out, 'fsdp', axis=0, tiled=True)  44 us
    all_gather x1, waiting for transfers between devices, per_device(): lax.all_gather(mlp_in, 'fsdp', axis=0, tiled=True)  38.7 us
    psum x1, blocking collectives, per_device(): grad_router = lax.psum(router_local, ('fsdp', 'dp'))  37.7 us
    dot_general x1, matrix products, per_device(): jnp.einsum('kf,kd->fd', active, grad_expanded, preferred_element_type=jnp...  18.8 us
    unnamed x1, blocking collectives  15.9 us
  transfers between devices with their start and end apart: 9, of which 6 were waited for; matrix products, arithmetic and copies ran while one was open for 26% of the time, Pallas kernels for 0%

commit v1 on v0

v1 whole, which is shorter than its diff:
```python
import numpy as np

import jax
import jax.numpy as jnp
from jax import lax
from jax.sharding import PartitionSpec as P

HEADS = 16
HEAD = 64


EPS = 1e-06
MASKED = -1e30


def rms_scale(values, gain_vec):
    return values * lax.rsqrt(jnp.mean(values * values, axis=-1, keepdims=True) + EPS) * gain_vec


def seq_mask(lengths, selected):
    seq_ends = jnp.cumsum(lengths)
    owner_seq = jnp.sum((selected[:, None] >= seq_ends[None, :]).astype(jnp.int32), axis=1)
    return (owner_seq[:, None] == owner_seq[None, :]) & (selected[None, :] <= selected[:, None])


def split_heads(matrix):
    return matrix.reshape(matrix.shape[0], HEADS, HEAD)


def masked_scores(query_heads, key_heads, allowed, score_scale):
    scores = (
        jnp.einsum("qhd,khd->hqk", query_heads, key_heads, preferred_element_type=jnp.float32)
        * score_scale
    )
    return jnp.where(allowed[None], scores, MASKED)


def plane_layout(mesh):
    devs = np.asarray(mesh.devices)
    if devs.ndim != 2 or devs.shape[0] != 8:
        return False
    try:
        for j in range(devs.shape[1]):
            for i in range(8):
                here = devs[i, j]
                mate = devs[i ^ 1, j]
                if tuple(mate.coords) != tuple(here.coords) or mate.core_on_chip == here.core_on_chip:
                    return False
                steps = []
                for bit in (2, 4):
                    other = devs[i ^ bit, j]
                    if other.core_on_chip != here.core_on_chip:
                        return False
                    diff = [abs(a - b) for a, b in zip(other.coords, here.coords)]
                    if sorted(diff) != [0] * (len(diff) - 1) + [1]:
                        return False
                    steps.append(diff.index(1))
                if steps[0] == steps[1]:
                    return False
    except AttributeError:
        return False
    return True


def swap_pairs(bit, size):
    return [(i, i ^ bit) for i in range(size)]


def plane_reduce(grad):
    rows, cols = grad.shape
    part = rows // 8
    half = part // 2
    me = lax.axis_index("fsdp")
    core = me % 2
    xi = (me // 2) % 2
    yi = me // 4
    blocks = grad.reshape(4, 2, part, cols)
    keep = lax.dynamic_index_in_dim(blocks, core, axis=1, keepdims=False)
    send = lax.dynamic_index_in_dim(blocks, 1 - core, axis=1, keepdims=False)
    got = lax.ppermute(send.astype(jnp.bfloat16), "fsdp", swap_pairs(1, 8))
    chip = keep + got.astype(jnp.float32)

    def pick(y, x):
        return lax.dynamic_index_in_dim(chip, y * 2 + x, axis=0, keepdims=False)

    own = pick(yi, xi)
    to_x = pick(yi, 1 - xi)
    to_y = pick(1 - yi, xi)
    to_d = pick(1 - yi, 1 - xi)
    first_x = lax.ppermute(
        jnp.stack([to_x[:half], to_d[:half]]).astype(jnp.bfloat16), "fsdp", swap_pairs(2, 8)
    ).astype(jnp.float32)
    first_y = lax.ppermute(
        jnp.stack([to_y[half:], to_d[half:]]).astype(jnp.bfloat16), "fsdp", swap_pairs(4, 8)
    ).astype(jnp.float32)
    own_a = own[:half] + first_x[0]
    pass_a = to_y[:half] + first_x[1]
    own_b = own[half:] + first_y[0]
    pass_b = to_x[half:] + first_y[1]
    second_y = lax.ppermute(pass_a.astype(jnp.bfloat16), "fsdp", swap_pairs(4, 8)).astype(jnp.float32)
    second_x = lax.ppermute(pass_b.astype(jnp.bfloat16), "fsdp", swap_pairs(2, 8)).astype(jnp.float32)
    shard = jnp.concatenate([own_a + second_y, own_b + second_x], axis=0)
    return lax.psum(shard.astype(jnp.bfloat16), "dp").astype(jnp.float32)


def plain_reduce(grad):
    shard = lax.psum_scatter(grad.astype(jnp.bfloat16), "fsdp", scatter_dimension=0, tiled=True)
    return lax.psum(shard, "dp").astype(jnp.float32)


def make_per_device(reduce_grad):
    def per_device(
        tokens,
        cotangent,
        lengths,
        selected,
        attn_in,
        attn_out,
        mlp_in,
        mlp_out,
        norm_attn,
        norm_mlp,
        router,
    ):
        model_width = tokens.shape[1]
        row_count = selected.shape[0]
        score_scale = HEAD ** (-0.5)
        w_qkv, gain_attn = (
            lax.all_gather(attn_in, "fsdp", axis=0, tiled=True),
            lax.all_gather(norm_attn, "fsdp", axis=0, tiled=True),
        )
        w_out = lax.all_gather(attn_out, "fsdp", axis=0, tiled=True)
        w_in, gain_mlp = (
            lax.all_gather(mlp_in, "fsdp", axis=0, tiled=True),
            lax.all_gather(norm_mlp, "fsdp", axis=0, tiled=True),
        )
        w_down = lax.all_gather(mlp_out, "fsdp", axis=0, tiled=True)
        gain_one = gain_attn.astype(jnp.float32)
        gain_two = gain_mlp.astype(jnp.float32)
        positions = lax.broadcasted_iota(jnp.int32, (row_count, tokens.shape[0]), 1)
        select = (selected[:, None] == positions).astype(jnp.bfloat16)
        routed = jnp.dot(select, tokens, preferred_element_type=jnp.float32)
        routed_low = routed.astype(jnp.bfloat16)
        router_rate = jnp.dot(routed_low, router, preferred_element_type=jnp.float32)
        allowed = seq_mask(lengths, selected)
        normed_float, norm_pull = jax.vjp(rms_scale, routed, gain_one)
        normed = normed_float.astype(jnp.bfloat16)
        qkv = jnp.dot(normed, w_qkv, preferred_element_type=jnp.float32).astype(jnp.bfloat16)
        query_heads = split_heads(qkv[:, :model_width])
        key_heads = split_heads(qkv[:, model_width : 2 * model_width])
        value_heads = split_heads(qkv[:, 2 * model_width :])
        scores = masked_scores(query_heads, key_heads, allowed, score_scale)
        highest = jnp.max(scores, axis=-1, keepdims=True)
        exponent = jnp.exp(scores - highest)
        row_total = jnp.sum(exponent, axis=-1, keepdims=True)
        probabilities = (exponent / row_total).astype(jnp.bfloat16)
        log_total = highest + jnp.log(row_total)
        attn_mix = jnp.einsum(
            "hqk,khd->qhd", probabilities, value_heads, preferred_element_type=jnp.float32
        )
        attn_mix = attn_mix.reshape(row_count, model_width).astype(jnp.bfloat16)
        attended = jnp.dot(attn_mix, w_out, preferred_element_type=jnp.float32)
        middle = routed + attended
        normed_two_float, middle_pull = jax.vjp(rms_scale, middle, gain_two)
        normed_two = normed_two_float.astype(jnp.bfloat16)
        pre_gelu = jnp.dot(normed_two, w_in, preferred_element_type=jnp.float32)
        active_float, gelu_pull = jax.vjp(jax.nn.gelu, pre_gelu)
        active = active_float.astype(jnp.bfloat16)
        expanded = jnp.dot(active, w_down, preferred_element_type=jnp.float32)
        update = attended + expanded
        branch = (router_rate[:, None] * update).astype(jnp.bfloat16)
        output = (
            tokens.astype(jnp.float32)
            + jnp.einsum("kt,kd->td", select, branch, preferred_element_type=jnp.float32)
        ).astype(jnp.bfloat16)
        cot_rows = jnp.dot(select, cotangent, preferred_element_type=jnp.float32)
        grad_rate = jnp.sum(cot_rows * update, axis=-1)
        grad_update = cot_rows * router_rate[:, None]
        grad_expanded = grad_update.astype(jnp.bfloat16)
        grad_down = jnp.einsum("kf,kd->fd", active, grad_expanded, preferred_element_type=jnp.float32)
        shard_down = reduce_grad(grad_down)
        grad_active = jnp.einsum(
            "kd,fd->kf", grad_expanded, w_down, preferred_element_type=jnp.float32
        )
        (grad_inner_float,) = gelu_pull(grad_active)
        grad_inner = grad_inner_float.astype(jnp.bfloat16)
        grad_up = jnp.einsum("kd,kf->df", normed_two, grad_inner, preferred_element_type=jnp.float32)
        shard_up = reduce_grad(grad_up)
        grad_normed_two = jnp.einsum(
            "kf,df->kd", grad_inner, w_in, preferred_element_type=jnp.float32
        )
        grad_middle, grad_gain_two = middle_pull(grad_normed_two)
        grad_attended = (grad_update + grad_middle).astype(jnp.bfloat16)
        grad_proj = jnp.einsum("ka,kd->ad", attn_mix, grad_attended, preferred_element_type=jnp.float32)
        shard_proj = reduce_grad(grad_proj)
        grad_mix = jnp.einsum(
            "kd,ad->ka", grad_attended, w_out, preferred_element_type=jnp.float32
        ).astype(jnp.bfloat16)
        grad_mix_heads = split_heads(grad_mix)
        scores_again = masked_scores(query_heads, key_heads, allowed, score_scale)
        prob_float = jnp.where(allowed[None], jnp.exp(scores_again - log_total), 0.0)
        grad_probs = jnp.einsum(
            "qhd,khd->hqk", grad_mix_heads, value_heads, preferred_element_type=jnp.float32
        )
        row_delta = jnp.sum(prob_float * grad_probs, axis=-1, keepdims=True)
        grad_scores = (prob_float * (grad_probs - row_delta)).astype(jnp.bfloat16)
        prob_low = prob_float.astype(jnp.bfloat16)
        grad_query = (
            jnp.einsum("hqk,khd->qhd", grad_scores, key_heads, preferred_element_type=jnp.float32)
            * score_scale
        )
        grad_key = (
            jnp.einsum("hqk,qhd->khd", grad_scores, query_heads, preferred_element_type=jnp.float32)
            * score_scale
        )
        grad_value = jnp.einsum(
            "hqk,qhd->khd", prob_low, grad_mix_heads, preferred_element_type=jnp.float32
        )
        grad_qkv = jnp.concatenate(
            [
                grad_query.reshape(row_count, model_width),
                grad_key.reshape(row_count, model_width),
                grad_value.reshape(row_count, model_width),
            ],
            axis=1,
        ).astype(jnp.bfloat16)
        grad_proj_in = jnp.einsum("kd,ke->de", normed, grad_qkv, preferred_element_type=jnp.float32)
        shard_qkv = reduce_grad(grad_proj_in)
        grad_normed = jnp.einsum("ke,de->kd", grad_qkv, w_qkv, preferred_element_type=jnp.float32)
        grad_routed_norm, grad_gain_one = norm_pull(grad_normed)
        grad_routed = (
            grad_routed_norm + grad_middle + grad_rate[:, None] * router.astype(jnp.float32)
        ).astype(jnp.bfloat16)
        grad_tokens = (
            cotangent.astype(jnp.float32)
            + jnp.einsum("kt,kd->td", select, grad_routed, preferred_element_type=jnp.float32)
        ).astype(jnp.bfloat16)
        router_local = jnp.dot(grad_rate, routed, precision=lax.Precision.HIGHEST)
        small = lax.psum(
            jnp.concatenate([grad_gain_one, grad_gain_two, router_local]), ("fsdp", "dp")
        )
        gain_part = grad_gain_one.shape[0] // lax.axis_size("fsdp")
        me = lax.axis_index("fsdp")
        shard_gain_one = lax.dynamic_slice_in_dim(small, me * gain_part, gain_part)
        shard_gain_two = lax.dynamic_slice_in_dim(
            small, grad_gain_one.shape[0] + me * gain_part, gain_part
        )
        grad_router = small[2 * grad_gain_one.shape[0] :]
        return (
            output,
            grad_tokens,
            shard_qkv,
            shard_proj,
            shard_up,
            shard_down,
            shard_gain_one,
            shard_gain_two,
            grad_router,
        )

    return per_device


def solution(mesh):
    placed = (
        P(("fsdp", "dp"), None),
        P(("fsdp", "dp"), None),
        P(("fsdp", "dp")),
        P(("fsdp", "dp")),
        P("fsdp", None),
        P("fsdp", None),
        P("fsdp", None),
        P("fsdp", None),
        P("fsdp"),
        P("fsdp"),
        P(),
    )
    reduce_grad = plane_reduce if plane_layout(mesh) else plain_reduce
    return jax.shard_map(
        make_per_device(reduce_grad),
        mesh=mesh,
        in_specs=placed,
        out_specs=(
            P(("fsdp", "dp"), None),
            P(("fsdp", "dp"), None),
            P("fsdp", None),
            P("fsdp", None),
            P("fsdp", None),
            P("fsdp", None),
            P("fsdp"),
            P("fsdp"),
            P(),
        ),
        check_vma=False,
    )
```

time: 783 us -> 648 us (0.83)
  waiting for transfers between devices: 412 us -> 241 us
  local copies, waits for them, and re-layouts: 14.3 us -> 43.2 us
  matrix products: 204 us -> 176 us
  other arithmetic: 44 us -> 71.7 us
  starting transfers between devices: 0.57 us -> 20.8 us
  blocking collectives: 84.6 us -> 71.3 us
    reduce_scatter x4 -> x0, waiting for transfers between devices: 217 us -> none  [the longest x1 117 us: per_device(): lax.psum_scatter(grad_up, 'fsdp', scatter_dimension=0, tiled=True)]
    ppermute x0 -> x20, waiting for transfers between devices: none -> 59.4 us  [the longest x4 43.6 us: plane_reduce(): lax.ppermute(jnp.stack([to_y[half:], to_d[half:]]).astype(jnp.bfloat16),...]
    ppermute x0 -> x20, starting transfers between devices: none -> 20.6 us  [the longest x4 6.99 us: plane_reduce(): lax.ppermute(pass_a.astype(jnp.bfloat16), 'fsdp', swap_pairs(4, 8))]
    add x0 -> x4, other arithmetic: none -> 20.5 us  [plane_reduce(): chip = keep + got.astype(jnp.float32)]
    unnamed x1 -> x0, blocking collectives: 15.9 us -> none
    convert_element_type x1 -> x5, local copies, waits for them, and re-layouts: 2.29 us -> 16.6 us  [the longest x4 14.3 us: plane_reduce(): got = lax.ppermute(send.astype(jnp.bfloat16), 'fsdp', swap_pairs(1, 8))]
    dot_general x1, matrix products: 18.8 us -> 9.27 us  [per_device(): jnp.einsum('kf,kd->fd', active, grad_expanded, preferred_element_type=jnp...]
    all_gather x2, waiting for transfers between devices: 44 us -> 35.3 us  [the longest x1 35.3 us: per_device(): w_down = lax.all_gather(mlp_out, 'fsdp', axis=0, tiled=True)]
  transfers between devices with their start and end apart: 9 -> 25, of which waited for: 6 -> 14; matrix products, arithmetic and copies ran while one was open for 26% -> 28% of each run, Pallas kernels for 0% -> 0%
where the time goes in v1:
time: 648 us; the launch traced here: 639 us
  waiting for transfers between devices  241 us (37%)
  matrix products  176 us (27%)
  other arithmetic  71.7 us (11%)
  blocking collectives  71.3 us (11%)
  local copies, waits for them, and re-layouts  43.2 us (7%)
  starting transfers between devices  20.8 us (3%)
  between operations  14.9 us (2%)
    psum x1, waiting for transfers between devices, plane_reduce(): return lax.psum(shard.astype(jnp.bfloat16), 'dp').astype(jnp.float32)  97.6 us
    psum x1, blocking collectives, per_device(): lax.psum(jnp.concatenate([grad_gain_one, grad_gain_two, router_local]), (...  52 us
    ppermute x4, waiting for transfers between devices, plane_reduce(): lax.ppermute(jnp.stack([to_y[half:], to_d[half:]]).astype(jnp.bfloat16),...  43.6 us
    all_gather x1, waiting for transfers between devices, per_device(): lax.all_gather(mlp_in, 'fsdp', axis=0, tiled=True)  38.5 us
    all_gather x1, waiting for transfers between devices, per_device(): w_down = lax.all_gather(mlp_out, 'fsdp', axis=0, tiled=True)  35.3 us
    add x4, other arithmetic, plane_reduce(): chip = keep + got.astype(jnp.float32)  20.5 us
    convert_element_type x4, local copies, waits for them, and re-layouts, plane_reduce(): got = lax.ppermute(send.astype(jnp.bfloat16), 'fsdp', swap_pairs(1, 8))  14.3 us
    dot_general x1, matrix products, per_device(): jnp.einsum('kd,fd->kf', grad_expanded, w_down, preferred_element_type=jnp...  13.6 us
  transfers between devices with their start and end apart: 25, of which 14 were waited for; matrix products, arithmetic and copies ran while one was open for 28% of the time, Pallas kernels for 0%

profile of v1, /device:TPU:0, one launch (start us, length us, event | category | flops | bytes accessed | tf_op | source)
XLA Modules:
  0.0 639.1 jit_solution(1268586833503978225)
XLA Ops:
  12.9 10.4 %all-gather = bf16[8,1,128]{2,1,0:T(2,128)(2,1)S(1)} all-gather(bf16[1,1,128]{2,1,0:T(2,128)(2,1)} %bitcast.194), channel_id=1, replica_groups=mesh['fsdp'=8,'dp'=4] {'fsdp'}, dimensions={0}, use_global_device_ids=true | all-gather | bytes 2304 | tf_op jit(solution)/shard_map/all_gather | solution.py:130
  23.3 8.8 %all-gather.1 = bf16[8,1,128]{2,1,0:T(2,128)(2,1)S(1)} all-gather(bf16[1,1,128]{2,1,0:T(2,128)(2,1)} %bitcast.195), channel_id=1, replica_groups=mesh['fsdp'=8,'dp'=4] {'fsdp'}, dimensions={0}, use_global_device_ids=true | all-gather | bytes 2304 | tf_op jit(solution)/shard_map/all_gather | solution.py:135
  41.4 9.3 %fusion.12 = f32[512,1024]{1,0:T(8,128)} fusion(bf16[4096,1024]{1,0:T(8,128)(2,1)} %param.12, s32[512]{0:T(512)S(1)} %copy-done.15), kind=kOutput, calls=%fused_computation.28 | convolution fusion | flops 4297064448 | bytes 10487808 | tf_op jit(solution)/shard_map/dot_general | solution.py:176
  72.4 8.9 %fusion.1 = (f32[16,512]{1,0:T(8,128)S(1)}, f32[16,512,512]{1,2,0:T(8,128)}) fusion(pred[512,512]{0,1:T(8,128)(4,1)S(1)} %compare_and_fusion, bf16[512,16,64]{0,2,1:T(8,128)(2,1)} %bitcast.161, bf16[512,16,64]{0,2,1:T(8,128)(2,1)S(1)} %bitcast.159), kind=kOutput, calls=%fused_computation.11 | convolution fusion | flops 549445632 | bytes 19169280 | tf_op jit(solution)/shard_map/qhd,khd->hqk/dot_general | solution.py:32
  81.3 9.3 %fusion = f32[16,512]{1,0:T(8,128)S(1)} fusion(f32[16,512,512]{1,2,0:T(8,128)} %get-tuple-element.61, f32[16,512]{1,0:T(8,128)S(1)} %get-tuple-element.60, pred[512,512]{0,1:T(8,128)(4,1)S(1)} %compare_and_fusion), kind=kLoop, calls=%fused_computation.8 | loop fusion | flops 16769024 | bytes 17104896 | tf_op jit(solution)/shard_map/reduce_sum | solution.py:155
  90.6 9.5 %fusion.26 = bf16[16,64,512]{2,1,0:T(8,128)(2,1)} fusion(bf16[512,16,64]{0,2,1:T(8,128)(2,1)} %bitcast.175, f32[16,512,512]{1,2,0:T(8,128)} %get-tuple-element.61, f32[16,512]{1,0:T(8,128)S(1)} %fusion, f32[16,512]{1,0:T(8,128)S(1)} %get-tuple-element.60, pred[512,512]{0,1:T(8,128)(4,1)S(1)} %compare_and_fusion), kind=kOutput, calls=%fused_computation.68 | convolution fusion | flops 558366720 | bytes 19202048 | tf_op jit(solution)/shard_map/hqk,khd->qhd/dot_general | solution.py:158
  105.4 38.5 %all-gather.11.cloned.1.call-done = bf16[1024,4096]{1,0:T(8,128)(2,1)} async-done(((bf16[128,4096]{1,0:T(8,128)(2,1)}), bf16[1024,4096]{1,0:T(8,128)(2,1)}) %all-gather.11.cloned.1.call-update) | async-done | bytes 8388624 | tf_op jit(solution)/shard_map/all_gather | solution.py:134
  155.4 9.3 %fusion.93 = f32[4096,1024]{1,0:T(8,128)} fusion(f32[512,1024]{1,0:T(8,128)S(1)} %copy-done.40, f32[512]{0:T(512)S(1)} %bitcast.189, f32[512,4096]{1,0:T(8,128)S(1)} %fusion.96), kind=kOutput, calls=%fused_computation.178 | convolution fusion | flops 4314890240 | bytes 27265024 | tf_op jit(solution)/shard_map/kf,kd->fd/dot_general | solution.py:180
  164.7 35.3 %all-gather.13.cloned.1.call-done = bf16[4096,1024]{1,0:T(8,128)(2,1)} async-done(((bf16[512,1024]{1,0:T(8,128)(2,1)}), bf16[4096,1024]{1,0:T(8,128)(2,1)}) %all-gather.13.cloned.1.call-update) | async-done | bytes 8388624 | tf_op jit(solution)/shard_map/all_gather | solution.py:137
  199.9 13.6 %fusion.8 = bf16[512,4096]{1,0:T(8,128)(2,1)S(1)} fusion(f32[512,4096]{1,0:T(8,128)} %copy-done.39, bf16[4096,1024]{1,0:T(8,128)(2,1)} %all-gather.13.cloned.1.call-done, f32[512,1024]{1,0:T(8,128)} %fusion.12, f32[512]{0:T(512)S(1)} %bitcast.190), kind=kOutput, calls=%fused_computation.18 | convolution fusion | flops 4337958912 | bytes 23070720 | tf_op jit(solution)/shard_map/kd,fd->kf/dot_general | solution.py:182
  215.6 8.4 %fusion.95 = f32[1024,4096]{1,0:T(8,128)} fusion(bf16[512,4096]{1,0:T(8,128)(2,1)S(1)} %fusion.8, f32[512,1024]{1,0:T(8,128)S(1)} %copy-done.4, f32[1024]{0:T(1024)S(1)} %bitcast.185, f32[512]{0:T(512)S(1)} %fusion.85), kind=kOutput, calls=%fused_computation.180 | convolution fusion | flops 4296540160 | bytes 23074816 | tf_op jit(solution)/shard_map/kd,kf->df/dot_general | solution.py:187
  223.9 11.5 %multiply_reduce_fusion.1 = (f32[1024]{0:T(1024)}, f32[512]{0:T(512)S(1)}, f32[512,1024]{1,0:T(8,128)}) fusion(f32[512,1024]{1,0:T(8,128)S(1)} %copy-done.4, f32[512]{0:T(512)S(1)} %fusion.85, f32[1024]{0:T(1024)S(1)} %bitcast.186, bf16[512,4096]{1,0:T(8,128)(2,1)} %copy-done.38, bf16[1024,4096]{1,0:T(8,128)(2,1)} %all-gather.11.cloned.1.call-done), kind=kOutput, calls=%fused_computation.49 | convolution fusion | flops 4298111488 | bytes 16789504 | tf_op jit(solution)/shard_map/kf,df->kd/dot_general | solution.py:189
  235.6 10.0 %multiply_reduce_fusion.3 = (f32[512]{0:T(512)S(1)}, bf16[512,1024]{1,0:T(8,128)(2,1)S(1)}, f32[512,1024]{1,0:T(8,128)}) fusion(f32[512,1024]{1,0:T(8,128)S(1)} %copy-done.41, f32[512,1024]{1,0:T(8,128)S(1)} %copy-done.4, f32[512]{0:T(512)S(1)} %multiply_multiply_fusion.3, f32[512]{0:T(512)S(1)} %fusion.85, f32[512,1024]{1,0:T(8,128)} %get-tuple-element.63, ...), kind=kOutput, calls=%fused_computation.54 | convolution fusion | flops 4319608320 | bytes 28323840 | tf_op jit(solution)/shard_map/dot_general | solution.py:169
  251.2 11.5 %fusion.27 = bf16[16,64,512]{2,1,0:T(8,128)(2,1)} fusion(bf16[512,16,64]{0,2,1:T(8,128)(2,1)} %bitcast.177, f32[16,512]{1,0:T(8,128)S(1)} %log_add_fusion, f32[16,512,512]{1,2,0:T(8,128)} %get-tuple-element.61, pred[512,512]{0,1:T(8,128)(4,1)S(1)} %compare_and_fusion), kind=kOutput, calls=%fused_computation.70 | convolution fusion | flops 558366720 | bytes 19169280 | tf_op jit(solution)/shard_map/hqk,qhd->khd/dot_general | solution.py:216
  262.7 12.5 %multiply_reduce_fusion = (f32[16,512]{1,0:T(8,128)S(1)}, f32[16,512,512]{1,2,0:T(8,128)}) fusion(f32[16,512]{1,0:T(8,128)S(1)} %log_add_fusion, f32[16,512,512]{1,2,0:T(8,128)} %get-tuple-element.61, pred[512,512]{0,1:T(8,128)(4,1)S(1)} %compare_and_fusion, bf16[512,16,64]{0,2,1:T(8,128)(2,1)S(1)} %bitcast.178, bf16[512,16,64]{0,2,1:T(8,128)(2,1)S(1)} %bitcast.176), kind=kOutput, calls=%fused_computation.2 | convolution fusion | flops 562028544 | bytes 35979264 | tf_op jit(solution)/shard_map/qhd,khd->hqk/dot_general | solution.py:202
  275.2 12.8 %multiply_convert_fusion = bf16[16,512,512]{1,2,0:T(8,128)(2,1)S(1)} fusion(f32[16,512,512]{1,2,0:T(8,128)} %get-tuple-element.66, f32[16,512]{1,0:T(8,128)S(1)} %get-tuple-element.65, f32[16,512]{1,0:T(8,128)S(1)} %log_add_fusion, f32[16,512,512]{1,2,0:T(8,128)} %get-tuple-element.61, pred[512,512]{0,1:T(8,128)(4,1)S(1)} %compare_and_fusion), kind=kLoop, calls=%fused_computation.1 | loop fusion | flops 29360128 | bytes 42270720 | tf_op jit(solution)/shard_map/convert_element_type | solution.py:206
  313.8 9.0 %multiply_reduce_fusion.2 = (f32[1024]{0:T(1024)}, f32[512]{0:T(512)S(1)}, f32[512,1024]{1,0:T(8,128)}) fusion(f32[512,1024]{1,0:T(8,128)S(1)} %get-tuple-element.59, f32[512]{0:T(512)S(1)} %copy-done.34, f32[1024]{0:T(1024)S(1)} %bitcast.182, bf16[1024,3072]{1,0:T(8,128)(2,1)} %all-gather.7.cloned.1.call-done, bf16[512,1024]{0,1:T(8,128)(2,1)} %bitcast.201, ...), kind=kOutput, calls=%fused_computation.50 | convolution fusion | flops 3233806848 | bytes 13643776 | tf_op jit(solution)/shard_map/ke,de->kd/dot_general | solution.py:229
  346.6 52.0 %psum.39 = f32[3072]{0:T(1024)} all-reduce(f32[3072]{0:T(1024)S(1)} %pad_maximum_fusion.15), channel_id=1, replica_groups=mesh['fsdp'=8,'dp'=4] {'fsdp','dp'}, use_global_device_ids=true, to_apply=%region_16.17 | all-reduce | flops 3072 | bytes 24576 | tf_op jit(solution)/shard_map/psum | solution.py:239
  419.8 10.3 %bitcast_add_fusion = f32[4,512,1024]{2,1,0:T(8,128)} fusion(bf16[4,512,1024]{2,1,0:T(8,128)(2,1)} %collective-permute-done.15, f32[4,2,512,1024]{3,2,1,0:T(8,128)} %bitcast.164, s32[]{:T(128)S(6)} %select_n.97), kind=kLoop, calls=%fused_computation.21 | loop fusion | flops 4194304 | bytes 20971524 | tf_op jit(solution)/shard_map/add | solution.py:81
  440.3 19.6 %collective-permute-done.18 = bf16[2,256,1024]{2,1,0:T(8,128)(2,1)S(1)} collective-permute-done((bf16[2,256,1024]{2,1,0:T(8,128)(2,1)S(1)}, bf16[2,256,1024]{2,1,0:T(8,128)(2,1)S(1)}, u32[]{:S(2)}, u32[]{:S(2)}) %collective-permute-start.18) | collective-permute-done | bytes 1048608 | tf_op jit(solution)/shard_map/ppermute | solution.py:93
  463.6 18.8 %collective-permute-done.13 = bf16[2,64,4096]{2,1,0:T(8,128)(2,1)S(1)} collective-permute-done((bf16[2,64,4096]{2,1,0:T(8,128)(2,1)S(1)}, bf16[2,64,4096]{2,1,0:T(8,128)(2,1)S(1)}, u32[]{:S(2)}, u32[]{:S(2)}) %collective-permute-start.13) | collective-permute-done | bytes 1048608 | tf_op jit(solution)/shard_map/ppermute | solution.py:93
  504.4 10.0 %add_convert_fusion.1 = bf16[4096,1024]{1,0:T(8,128)(2,1)} fusion(bf16[4096,1024]{1,0:T(8,128)(2,1)} %param.11, s32[512]{0:T(512)S(1)} %copy-done.16, f32[512,1024]{1,0:T(8,128)} %get-tuple-element.64, f32[512]{0:T(512)S(1)} %bitcast.192), kind=kOutput, calls=%fused_computation.4 | convolution fusion | flops 4310695936 | bytes 18878464 | tf_op jit(solution)/shard_map/kt,kd->td/dot_general | solution.py:174
  514.5 11.6 %add_convert_fusion = bf16[4096,1024]{1,0:T(8,128)(2,1)} fusion(bf16[4096,1024]{1,0:T(8,128)(2,1)} %param.12, s32[512]{0:T(512)S(1)} %copy-done.16, f32[512,1024]{1,0:T(8,128)S(1)} %get-tuple-element.59, f32[512,1024]{1,0:T(8,128)S(1)} %copy-done.42, f32[1024]{0:T(1024)S(1)} %copy-done.19, f32[512]{0:T(512)S(1)} %copy-done.29, f32[512]{0:T(512)S(1)} %copy-done.32, ...), kind=kOutput, calls=%fused_computation | convolution fusion | flops 4316987392 | bytes 25190400 | tf_op jit(solution)/shard_map/kt,kd->td/dot_general | solution.py:236
  526.1 97.6 %all-reduce.3.cloned.1.call-done = (bf16[128,3072]{1,0:T(8,128)(2,1)}, bf16[128,1024]{1,0:T(8,128)(2,1)}, bf16[128,4096]{1,0:T(8,128)(2,1)}, bf16[512,1024]{1,0:T(8,128)(2,1)}) async-done(((bf16[128,3072]{1,0:T(8,128)(2,1)}, bf16[128,1024]{1,0:T(8,128)(2,1)}, bf16[128,4096]{1,0:T(8,128)(2,1)}, bf16[512,1024]{1,0:T(8,128)(2,1)}), (bf16[128,3072]{1,0:T(8,128)(2,1)}, bf16[128,1024]{1,0:T(8,128)(2,1)}, ...) | async-done | bytes 3145744 | tf_op jit(solution)/shard_map/psum | solution.py:103
  (230 shorter events, 175.8 us)
Async XLA Ops:
  7.2 50.9 %all-gather.7.cloned.1.call-start = ((), (), s32[]{:S(2)}) async-start(), calls=%async_computation | async-start | bytes 7077888 | tf_op jit(solution)/shard_map/all_gather | solution.py:129
  7.9 92.2 %all-gather.9.cloned.1.call-start = ((), (), s32[]{:S(2)}) async-start(), calls=%async_computation.1 | async-start | bytes 2359296 | tf_op jit(solution)/shard_map/all_gather | solution.py:132
  8.7 135.2 %all-gather.11.cloned.1.call-start = ((), (), s32[]{:S(2)}) async-start(), calls=%async_computation.2 | async-start | bytes 9437184 | tf_op jit(solution)/shard_map/all_gather | solution.py:134
  9.4 190.5 %all-gather.13.cloned.1.call-start = ((), (), s32[]{:S(2)}) async-start(), calls=%async_computation.3 | async-start | bytes 9437184 | tf_op jit(solution)/shard_map/all_gather | solution.py:137
  10.0 613.7 %all-reduce.3.cloned.1.call-start = ((), (), s32[]{:S(2)}) async-start(), calls=%async_computation.4 | async-start | bytes 6291456 | tf_op jit(solution)/shard_map/psum | solution.py:103
  293.6 29.2 %collective-permute-start.5 = (bf16[4,128,1024]{2,1,0:T(8,128)(2,1)S(1)}, bf16[4,128,1024]{2,1,0:T(8,128)(2,1)}, u32[]{:S(2)}, u32[]{:S(2)}) collective-permute-start(bf16[4,128,1024]{2,1,0:T(8,128)(2,1)S(1)} %fusion.32), channel_id=1, source_target_pairs={{0,4},{4,0},{8,12},{12,8},{16,20},{20,16},{24,28},{28,24},{1,5},{5... | collective-permute-start | bytes 3145736 | tf_op jit(solution)/shard_map/ppermute | solution.py:80
  299.9 119.8 %collective-permute-start.15 = (bf16[4,512,1024]{2,1,0:T(8,128)(2,1)}, bf16[4,512,1024]{2,1,0:T(8,128)(2,1)}, u32[]{:S(2)}, u32[]{:S(2)}) collective-permute-start(bf16[4,512,1024]{2,1,0:T(8,128)(2,1)} %fusion.17), channel_id=1, source_target_pairs={{0,4},{4,0},{8,12},{12,8},{16,20},{20,16},{24,28},{28,24},{1,5},{5... | collective-permute-start | bytes 12582920 | tf_op jit(solution)/shard_map/ppermute | solution.py:80
  307.3 27.8 %collective-permute-start = (bf16[4,128,3072]{2,1,0:T(8,128)(2,1)}, bf16[4,128,3072]{2,1,0:T(8,128)(2,1)}, u32[]{:S(2)}, u32[]{:S(2)}) collective-permute-start(bf16[4,128,3072]{2,1,0:T(8,128)(2,1)} %fusion.22), channel_id=1, source_target_pairs={{0,4},{4,0},{8,12},{12,8},{16,20},{20,16},{24,28},{28,24},{1,5},{5... | collective-permute-start | bytes 9437192 | tf_op jit(solution)/shard_map/ppermute | solution.py:80
  313.6 98.4 %collective-permute-start.10 = (bf16[4,128,4096]{2,1,0:T(8,128)(2,1)}, bf16[4,128,4096]{2,1,0:T(8,128)(2,1)}, u32[]{:S(2)}, u32[]{:S(2)}) collective-permute-start(bf16[4,128,4096]{2,1,0:T(8,128)(2,1)} %fusion.16), channel_id=1, source_target_pairs={{0,4},{4,0},{8,12},{12,8},{16,20},{20,16},{24,28},{28,24},{1,5},{5... | collective-permute-start | bytes 12582920 | tf_op jit(solution)/shard_map/ppermute | solution.py:80
  324.5 8.5 %collective-permute-start.8 = (bf16[2,64,1024]{2,1,0:T(8,128)(2,1)S(1)}, bf16[2,64,1024]{2,1,0:T(8,128)(2,1)S(1)}, u32[]{:S(2)}, u32[]{:S(2)}) collective-permute-start(bf16[2,64,1024]{2,1,0:T(8,128)(2,1)S(1)} %pad_maximum_fusion.13), channel_id=1, source_target_pairs={{0,16},{4,20},{8,24},{12,28},{16,0},{20,4},{24,8},{28,12},{1,17},{... | collective-permute-start | bytes 786440 | tf_op jit(solution)/shard_map/ppermute | solution.py:93
  334.1 11.3 %collective-permute-start.7 = (bf16[64,1024]{1,0:T(8,128)(2,1)S(1)}, bf16[64,1024]{1,0:T(8,128)(2,1)S(1)}, u32[]{:S(2)}, u32[]{:S(2)}) collective-permute-start(bf16[64,1024]{1,0:T(8,128)(2,1)S(1)} %get-tuple-element.42), channel_id=1, source_target_pairs={{0,16},{4,20},{8,24},{12,28},{16,0},{20,4},{24,8},{28,12},{1,17},{... | collective-permute-start | bytes 393224 | tf_op jit(solution)/shard_map/ppermute | solution.py:100
  341.9 61.2 %collective-permute-start.3 = (bf16[2,64,3072]{2,1,0:T(8,128)(2,1)}, bf16[2,64,3072]{2,1,0:T(8,128)(2,1)}, u32[]{:S(2)}, u32[]{:S(2)}) collective-permute-start(bf16[2,64,3072]{2,1,0:T(8,128)(2,1)} %pad_maximum_fusion.10), channel_id=1, source_target_pairs={{0,16},{4,20},{8,24},{12,28},{16,0},{20,4},{24,8},{28,12},{1,17},{... | collective-permute-start | bytes 2359304 | tf_op jit(solution)/shard_map/ppermute | solution.py:93
  343.9 60.4 %collective-permute-start.1 = (bf16[2,64,3072]{2,1,0:T(8,128)(2,1)}, bf16[2,64,3072]{2,1,0:T(8,128)(2,1)}, u32[]{:S(2)}, u32[]{:S(2)}) collective-permute-start(bf16[2,64,3072]{2,1,0:T(8,128)(2,1)} %pad_maximum_fusion.9), channel_id=1, source_target_pairs={{0,8},{4,12},{8,0},{12,4},{16,24},{20,28},{24,16},{28,20},{1,9},{5... | collective-permute-start | bytes 2359304 | tf_op jit(solution)/shard_map/ppermute | solution.py:90
  345.4 55.7 %collective-permute-start.9 = (bf16[64,1024]{1,0:T(8,128)(2,1)S(1)}, bf16[64,1024]{1,0:T(8,128)(2,1)S(1)}, u32[]{:S(2)}, u32[]{:S(2)}) collective-permute-start(bf16[64,1024]{1,0:T(8,128)(2,1)S(1)} %get-tuple-element.43), channel_id=1, source_target_pairs={{0,8},{4,12},{8,0},{12,4},{16,24},{20,28},{24,16},{28,20},{1,9},{5... | collective-permute-start | bytes 393224 | tf_op jit(solution)/shard_map/ppermute | solution.py:101
  408.1 29.2 %collective-permute-start.2 = (bf16[64,3072]{1,0:T(8,128)(2,1)}, bf16[64,3072]{1,0:T(8,128)(2,1)S(1)}, u32[]{:S(2)}, u32[]{:S(2)}) collective-permute-start(bf16[64,3072]{1,0:T(8,128)(2,1)} %get-tuple-element.33), channel_id=1, source_target_pairs={{0,16},{4,20},{8,24},{12,28},{16,0},{20,4},{24,8},{28,12},{1,17},{... | collective-permute-start | bytes 1179656 | tf_op jit(solution)/shard_map/ppermute | solution.py:100
  410.8 27.8 %collective-permute-start.4 = (bf16[64,3072]{1,0:T(8,128)(2,1)}, bf16[64,3072]{1,0:T(8,128)(2,1)}, u32[]{:S(2)}, u32[]{:S(2)}) collective-permute-start(bf16[64,3072]{1,0:T(8,128)(2,1)} %get-tuple-element.34), channel_id=1, source_target_pairs={{0,8},{4,12},{8,0},{12,4},{16,24},{20,28},{24,16},{28,20},{1,9},{5... | collective-permute-start | bytes 1179656 | tf_op jit(solution)/shard_map/ppermute | solution.py:101
  433.8 26.1 %collective-permute-start.18 = (bf16[2,256,1024]{2,1,0:T(8,128)(2,1)S(1)}, bf16[2,256,1024]{2,1,0:T(8,128)(2,1)S(1)}, u32[]{:S(2)}, u32[]{:S(2)}) collective-permute-start(bf16[2,256,1024]{2,1,0:T(8,128)(2,1)S(1)} %pad_maximum_fusion.7), channel_id=1, source_target_pairs={{0,16},{4,20},{8,24},{12,28},{16,0},{20,4},{24,8},{28,12},{1,17},{... | collective-permute-start | bytes 3145736 | tf_op jit(solution)/shard_map/ppermute | solution.py:93
  434.4 26.1 %collective-permute-start.16 = (bf16[2,256,1024]{2,1,0:T(8,128)(2,1)S(1)}, bf16[2,256,1024]{2,1,0:T(8,128)(2,1)S(1)}, u32[]{:S(2)}, u32[]{:S(2)}) collective-permute-start(bf16[2,256,1024]{2,1,0:T(8,128)(2,1)S(1)} %pad_maximum_fusion.6), channel_id=1, source_target_pairs={{0,8},{4,12},{8,0},{12,4},{16,24},{20,28},{24,16},{28,20},{1,9},{5... | collective-permute-start | bytes 3145736 | tf_op jit(solution)/shard_map/ppermute | solution.py:90
  435.1 47.2 %collective-permute-start.13 = (bf16[2,64,4096]{2,1,0:T(8,128)(2,1)S(1)}, bf16[2,64,4096]{2,1,0:T(8,128)(2,1)S(1)}, u32[]{:S(2)}, u32[]{:S(2)}) collective-permute-start(bf16[2,64,4096]{2,1,0:T(8,128)(2,1)S(1)} %pad_maximum_fusion.4), channel_id=1, source_target_pairs={{0,16},{4,20},{8,24},{12,28},{16,0},{20,4},{24,8},{28,12},{1,17},{... | collective-permute-start | bytes 3145736 | tf_op jit(solution)/shard_map/ppermute | solution.py:93
  437.3 45.6 %collective-permute-start.11 = (bf16[2,64,4096]{2,1,0:T(8,128)(2,1)S(1)}, bf16[2,64,4096]{2,1,0:T(8,128)(2,1)S(1)}, u32[]{:S(2)}, u32[]{:S(2)}) collective-permute-start(bf16[2,64,4096]{2,1,0:T(8,128)(2,1)S(1)} %pad_maximum_fusion.3), channel_id=1, source_target_pairs={{0,8},{4,12},{8,0},{12,4},{16,24},{20,28},{24,16},{28,20},{1,9},{5... | collective-permute-start | bytes 3145736 | tf_op jit(solution)/shard_map/ppermute | solution.py:90
  461.1 32.5 %collective-permute-start.17 = (bf16[256,1024]{1,0:T(8,128)(2,1)S(1)}, bf16[256,1024]{1,0:T(8,128)(2,1)S(1)}, u32[]{:S(2)}, u32[]{:S(2)}) collective-permute-start(bf16[256,1024]{1,0:T(8,128)(2,1)S(1)} %get-tuple-element.21), channel_id=1, source_target_pairs={{0,16},{4,20},{8,24},{12,28},{16,0},{20,4},{24,8},{28,12},{1,17},{... | collective-permute-start | bytes 1572872 | tf_op jit(solution)/shard_map/ppermute | solution.py:100
  462.7 31.5 %collective-permute-start.19 = (bf16[256,1024]{1,0:T(8,128)(2,1)S(1)}, bf16[256,1024]{1,0:T(8,128)(2,1)S(1)}, u32[]{:S(2)}, u32[]{:S(2)}) collective-permute-start(bf16[256,1024]{1,0:T(8,128)(2,1)S(1)} %get-tuple-element.22), channel_id=1, source_target_pairs={{0,8},{4,12},{8,0},{12,4},{16,24},{20,28},{24,16},{28,20},{1,9},{5... | collective-permute-start | bytes 1572872 | tf_op jit(solution)/shard_map/ppermute | solution.py:101
  483.4 18.3 %collective-permute-start.12 = (bf16[64,4096]{1,0:T(8,128)(2,1)S(1)}, bf16[64,4096]{1,0:T(8,128)(2,1)S(1)}, u32[]{:S(2)}, u32[]{:S(2)}) collective-permute-start(bf16[64,4096]{1,0:T(8,128)(2,1)S(1)} %get-tuple-element.27), channel_id=1, source_target_pairs={{0,16},{4,20},{8,24},{12,28},{16,0},{20,4},{24,8},{28,12},{1,17},{... | collective-permute-start | bytes 1572872 | tf_op jit(solution)/shard_map/ppermute | solution.py:100
  485.1 17.7 %collective-permute-start.14 = (bf16[64,4096]{1,0:T(8,128)(2,1)S(1)}, bf16[64,4096]{1,0:T(8,128)(2,1)S(1)}, u32[]{:S(2)}, u32[]{:S(2)}) collective-permute-start(bf16[64,4096]{1,0:T(8,128)(2,1)S(1)} %get-tuple-element.28), channel_id=1, source_target_pairs={{0,8},{4,12},{8,0},{12,4},{16,24},{20,28},{24,16},{28,20},{1,9},{5... | collective-permute-start | bytes 1572872 | tf_op jit(solution)/shard_map/ppermute | solution.py:101
  (49 other events, 1061.0 us)
Sparse Core Ops, SparseCore 0:
  9.9 48.1 all-gather.6
  59.9 27.7 all-gather.8
  89.6 54.2 all-gather.10
  145.6 54.2 all-gather.12
  504.3 119.2 all-reduce.2
